TPU v7x, 256 devices: a whole 4x4x8 slice. The times are simulated.
256 devices in a mesh: blk: 64 (over y, x_lo, z), team: 4 (over x_hi, core).
Axes of the slice: x: 4 (x_hi: 2, x_lo: 2; x = x_hi * 2 + x_lo), y: 4, z: 8, core: 2. Of those that a mesh axis runs over, the one named last changes fastest.
Arguments:
- loadings: bfloat16 [64, 98304], P(None, ('blk', 'team')), may hold values from -6 to 6
- scales: bfloat16 [64, 768], P(None, ('blk', 'team')), may hold values from 0.25 to 4
- cov: bfloat16 [16384, 16, 4, 1536], P('blk', None, 'team'), may hold values from -0.01953125 to 0.01953125
Outputs:
- product: float32 [64, 16384], P(None, 'blk')
All inputs are finite; a program needn't handle non-finite values.
Results may differ from a plain program's by a relative error of at most 0.0028.
Values may be sent and summed in bfloat16 or wider, within the bound.
No kernel may reach another device: no remote copies, remote signals or barrier semaphores. Data moves between devices by JAX's collectives and lax.ppermute only.
A program may use at most 128 MiB of HBM per device.

v0:
```python
import jax
import jax.numpy as jnp
from jax import lax
from jax.sharding import PartitionSpec as P


def passed_along(x, axis, by):
    size = lax.axis_size(axis)
    return lax.ppermute(x, axis, [(i, (i + by) % size) for i in range(size)])


def per_device(loadings, scales, cov):
    team_size = lax.axis_size("team")
    cycle_size = lax.axis_size("blk")
    cycle_stops = cycle_size // team_size
    cycle_pos = lax.axis_index("blk")
    member = lax.axis_index("team")
    skew_lag = jnp.mod(cycle_pos - member, team_size)
    base_stop = jnp.mod((cycle_pos - skew_lag - member) // team_size, cycle_stops)
    held_block = (
        lax.all_gather(loadings, "team", axis=1, tiled=True),
        lax.all_gather(scales, "team", axis=1, tiled=True),
    )
    near_copy = passed_along((held_block[0], held_block[1]), "blk", 1)
    far_copies = passed_along((held_block[0], held_block[1], near_copy[0], near_copy[1]), "blk", 2)
    stacked_loads = jnp.stack([held_block[0], near_copy[0], far_copies[0], far_copies[2]])
    stacked_scales = jnp.stack([held_block[1], near_copy[1], far_copies[1], far_copies[3]])
    start_block = (
        lax.dynamic_index_in_dim(stacked_loads, skew_lag, 0, keepdims=False),
        lax.dynamic_index_in_dim(stacked_scales, skew_lag, 0, keepdims=False),
    )
    cov_local = cov[:, :, 0, :]
    n_loads = loadings.shape[0]
    row_count = cov.shape[0]

    def contribute(running, block, stop_num):
        block_load, block_scale = block
        groups = block_scale.shape[1]
        scaled = (
            (
                block_load.astype(jnp.float32).reshape(
                    n_loads, groups, block_load.shape[1] // groups
                )
                * block_scale.astype(jnp.float32)[:, :, None]
            )
            .reshape(n_loads, block_load.shape[1])
            .astype(jnp.bfloat16)
        )
        cov_slab = lax.dynamic_index_in_dim(
            cov_local, jnp.mod(stop_num, cycle_stops), 1, keepdims=False
        )
        term = lax.dot_general(
            scaled, cov_slab, (((1,), (1,)), ((), ())), preferred_element_type=jnp.float32
        )
        return running + term

    initial = jnp.zeros((n_loads, row_count), jnp.float32)
    running = contribute(initial, start_block, base_stop)

    def onward(stop_num, carry):
        partial_sum, moving = carry
        moving = passed_along((moving[0], moving[1]), "blk", team_size)
        return (contribute(partial_sum, moving, base_stop - stop_num), moving)

    running, _ = lax.fori_loop(1, cycle_stops, onward, (running, start_block))
    product = lax.psum(running, "team")
    return product


def solution(mesh):
    placed = (P(None, ("blk", "team")), P(None, ("blk", "team")), P("blk", None, "team", None))
    return jax.shard_map(
        per_device, mesh=mesh, in_specs=placed, out_specs=P(None, "blk"), check_vma=False
    )
```

profile of v0, /device:TPU:1, one launch (start us, length us, event | category | flops | bytes accessed | tf_op | source)
XLA Modules:
  0.0 371.3 jit_solution(5446585981449639470)
XLA Ops:
  6.5 10.4 %all_gather.6 = bf16[64,1536]{1,0:T(8,128)(2,1)S(1)} all-gather(bf16[64,384]{1,0:T(8,128)(2,1)} %param.5), channel_id=1, replica_groups=mesh['blk'=64,'team'=4] {'team'}, dimensions={1}, use_global_device_ids=true | all-gather | bytes 245760 | tf_op jit(solution)/shard_map/all_gather | solution.py:21
  19.8 7.4 %all-gather = bf16[4,3,64]{2,1,0:T(4,128)(2,1)S(1)} all-gather(bf16[1,3,64]{2,1,0:T(4,128)(2,1)} %bitcast.55), channel_id=1, replica_groups=mesh['blk'=64,'team'=4] {'team'}, dimensions={0}, use_global_device_ids=true | all-gather | bytes 1920 | tf_op jit(solution)/shard_map/all_gather | solution.py:22
  31.2 6.3 %collective-permute-done.5 = bf16[64,12]{0,1:T(8,128)(2,1)S(1)} collective-permute-done((bf16[64,12]{0,1:T(8,128)(2,1)S(1)}, bf16[64,12]{0,1:T(8,128)(2,1)S(1)}, u32[]{:S(2)}, u32[]{:S(2)}) %collective-permute-start.5) | collective-permute-done | bytes 1568 | tf_op jit(solution)/shard_map/ppermute | solution.py:9
  42.7 13.0 %copy.27 = bf16[256,16,1,1536]{3,0,1,2:T(8,128)(2,1)} copy(bf16[256,16,1,1536]{3,1,2,0:T(8,128)(2,1)} %param.7) | data formatting | bytes 25165824 | tf_op args[2]
  56.8 219.6 %while.19 = (s32[]{:T(128)}, f32[64,256]{1,0:T(8,128)S(1)}, bf16[64,1536]{1,0:T(8,128)(2,1)S(1)}, bf16[64,12]{1,0:T(8,128)(2,1)S(1)}, s32[]{:T(128)}, /*index=5*...) while((s32[]{:T(128)}, f32[64,256]{1,0:T(8,128)S(1)}, ...), condition=%wide.region_1.2_spmd, body=%wide.region_0.1_spmd.sunk | while | flops 50642960 | bytes 3091284 | solution.py:65
  63.2 8.5 %collective-permute-done = bf16[64,12]{1,0:T(8,128)(2,1)S(1)} collective-permute-done((bf16[64,12]{1,0:T(8,128)(2,1)S(1)}, bf16[64,12]{1,0:T(8,128)(2,1)S(1)}, u32[]{:S(2)}, u32[]{:S(2)}) %collective-permute-start) | collective-permute-done | bytes 1568 | tf_op jit(solution)/shard_map/while/body/eval_jaxpr/ppermute | solution.py:9
  74.2 5.7 %collective-permute-start = (bf16[64,12]{1,0:T(8,128)(2,1)S(1)}, bf16[64,12]{1,0:T(8,128)(2,1)S(1)}, u32[]{:S(2)}, u32[]{:S(2)}) collective-permute-start(bf16[64,12]{1,0:T(8,128)(2,1)S(1)} %get-tuple-element.235), channel_id=1, source_target_pairs={{0,16},{4,20},{8,24},{12,28},{16,32},{20,36},{24,40},{28,44},{32,4... | collective-permute-start | bytes 4616 | tf_op jit(solution)/shard_map/while/body/eval_jaxpr/ppermute | solution.py:9
  79.9 11.1 %collective-permute-done = bf16[64,12]{1,0:T(8,128)(2,1)S(1)} collective-permute-done((bf16[64,12]{1,0:T(8,128)(2,1)S(1)}, bf16[64,12]{1,0:T(8,128)(2,1)S(1)}, u32[]{:S(2)}, u32[]{:S(2)}) %collective-permute-start) | collective-permute-done | bytes 1568 | tf_op jit(solution)/shard_map/while/body/eval_jaxpr/ppermute | solution.py:9
  94.8 10.4 %collective-permute-done = bf16[64,12]{1,0:T(8,128)(2,1)S(1)} collective-permute-done((bf16[64,12]{1,0:T(8,128)(2,1)S(1)}, bf16[64,12]{1,0:T(8,128)(2,1)S(1)}, u32[]{:S(2)}, u32[]{:S(2)}) %collective-permute-start) | collective-permute-done | bytes 1568 | tf_op jit(solution)/shard_map/while/body/eval_jaxpr/ppermute | solution.py:9
  110.6 8.2 %collective-permute-done = bf16[64,12]{1,0:T(8,128)(2,1)S(1)} collective-permute-done((bf16[64,12]{1,0:T(8,128)(2,1)S(1)}, bf16[64,12]{1,0:T(8,128)(2,1)S(1)}, u32[]{:S(2)}, u32[]{:S(2)}) %collective-permute-start) | collective-permute-done | bytes 1568 | tf_op jit(solution)/shard_map/while/body/eval_jaxpr/ppermute | solution.py:9
  125.2 7.1 %collective-permute-done = bf16[64,12]{1,0:T(8,128)(2,1)S(1)} collective-permute-done((bf16[64,12]{1,0:T(8,128)(2,1)S(1)}, bf16[64,12]{1,0:T(8,128)(2,1)S(1)}, u32[]{:S(2)}, u32[]{:S(2)}) %collective-permute-start) | collective-permute-done | bytes 1568 | tf_op jit(solution)/shard_map/while/body/eval_jaxpr/ppermute | solution.py:9
  134.1 5.4 %collective-permute-start = (bf16[64,12]{1,0:T(8,128)(2,1)S(1)}, bf16[64,12]{1,0:T(8,128)(2,1)S(1)}, u32[]{:S(2)}, u32[]{:S(2)}) collective-permute-start(bf16[64,12]{1,0:T(8,128)(2,1)S(1)} %get-tuple-element.235), channel_id=1, source_target_pairs={{0,16},{4,20},{8,24},{12,28},{16,32},{20,36},{24,40},{28,44},{32,4... | collective-permute-start | bytes 4616 | tf_op jit(solution)/shard_map/while/body/eval_jaxpr/ppermute | solution.py:9
  139.5 6.3 %collective-permute-done = bf16[64,12]{1,0:T(8,128)(2,1)S(1)} collective-permute-done((bf16[64,12]{1,0:T(8,128)(2,1)S(1)}, bf16[64,12]{1,0:T(8,128)(2,1)S(1)}, u32[]{:S(2)}, u32[]{:S(2)}) %collective-permute-start) | collective-permute-done | bytes 1568 | tf_op jit(solution)/shard_map/while/body/eval_jaxpr/ppermute | solution.py:9
  147.8 6.4 %collective-permute-start = (bf16[64,12]{1,0:T(8,128)(2,1)S(1)}, bf16[64,12]{1,0:T(8,128)(2,1)S(1)}, u32[]{:S(2)}, u32[]{:S(2)}) collective-permute-start(bf16[64,12]{1,0:T(8,128)(2,1)S(1)} %get-tuple-element.235), channel_id=1, source_target_pairs={{0,16},{4,20},{8,24},{12,28},{16,32},{20,36},{24,40},{28,44},{32,4... | collective-permute-start | bytes 4616 | tf_op jit(solution)/shard_map/while/body/eval_jaxpr/ppermute | solution.py:9
  154.2 5.0 %collective-permute-done = bf16[64,12]{1,0:T(8,128)(2,1)S(1)} collective-permute-done((bf16[64,12]{1,0:T(8,128)(2,1)S(1)}, bf16[64,12]{1,0:T(8,128)(2,1)S(1)}, u32[]{:S(2)}, u32[]{:S(2)}) %collective-permute-start) | collective-permute-done | bytes 1568 | tf_op jit(solution)/shard_map/while/body/eval_jaxpr/ppermute | solution.py:9
  165.6 7.0 %collective-permute-done = bf16[64,12]{1,0:T(8,128)(2,1)S(1)} collective-permute-done((bf16[64,12]{1,0:T(8,128)(2,1)S(1)}, bf16[64,12]{1,0:T(8,128)(2,1)S(1)}, u32[]{:S(2)}, u32[]{:S(2)}) %collective-permute-start) | collective-permute-done | bytes 1568 | tf_op jit(solution)/shard_map/while/body/eval_jaxpr/ppermute | solution.py:9
  177.0 10.0 %collective-permute-done = bf16[64,12]{1,0:T(8,128)(2,1)S(1)} collective-permute-done((bf16[64,12]{1,0:T(8,128)(2,1)S(1)}, bf16[64,12]{1,0:T(8,128)(2,1)S(1)}, u32[]{:S(2)}, u32[]{:S(2)}) %collective-permute-start) | collective-permute-done | bytes 1568 | tf_op jit(solution)/shard_map/while/body/eval_jaxpr/ppermute | solution.py:9
  190.2 12.2 %collective-permute-done = bf16[64,12]{1,0:T(8,128)(2,1)S(1)} collective-permute-done((bf16[64,12]{1,0:T(8,128)(2,1)S(1)}, bf16[64,12]{1,0:T(8,128)(2,1)S(1)}, u32[]{:S(2)}, u32[]{:S(2)}) %collective-permute-start) | collective-permute-done | bytes 1568 | tf_op jit(solution)/shard_map/while/body/eval_jaxpr/ppermute | solution.py:9
  204.3 13.2 %collective-permute-done = bf16[64,12]{1,0:T(8,128)(2,1)S(1)} collective-permute-done((bf16[64,12]{1,0:T(8,128)(2,1)S(1)}, bf16[64,12]{1,0:T(8,128)(2,1)S(1)}, u32[]{:S(2)}, u32[]{:S(2)}) %collective-permute-start) | collective-permute-done | bytes 1568 | tf_op jit(solution)/shard_map/while/body/eval_jaxpr/ppermute | solution.py:9
  219.4 14.1 %collective-permute-done = bf16[64,12]{1,0:T(8,128)(2,1)S(1)} collective-permute-done((bf16[64,12]{1,0:T(8,128)(2,1)S(1)}, bf16[64,12]{1,0:T(8,128)(2,1)S(1)}, u32[]{:S(2)}, u32[]{:S(2)}) %collective-permute-start) | collective-permute-done | bytes 1568 | tf_op jit(solution)/shard_map/while/body/eval_jaxpr/ppermute | solution.py:9
  235.5 12.3 %collective-permute-done = bf16[64,12]{1,0:T(8,128)(2,1)S(1)} collective-permute-done((bf16[64,12]{1,0:T(8,128)(2,1)S(1)}, bf16[64,12]{1,0:T(8,128)(2,1)S(1)}, u32[]{:S(2)}, u32[]{:S(2)}) %collective-permute-start) | collective-permute-done | bytes 1568 | tf_op jit(solution)/shard_map/while/body/eval_jaxpr/ppermute | solution.py:9
  250.1 11.1 %collective-permute-done = bf16[64,12]{1,0:T(8,128)(2,1)S(1)} collective-permute-done((bf16[64,12]{1,0:T(8,128)(2,1)S(1)}, bf16[64,12]{1,0:T(8,128)(2,1)S(1)}, u32[]{:S(2)}, u32[]{:S(2)}) %collective-permute-start) | collective-permute-done | bytes 1568 | tf_op jit(solution)/shard_map/while/body/eval_jaxpr/ppermute | solution.py:9
  264.2 10.6 %collective-permute-done = bf16[64,12]{1,0:T(8,128)(2,1)S(1)} collective-permute-done((bf16[64,12]{1,0:T(8,128)(2,1)S(1)}, bf16[64,12]{1,0:T(8,128)(2,1)S(1)}, u32[]{:S(2)}, u32[]{:S(2)}) %collective-permute-start) | collective-permute-done | bytes 1568 | tf_op jit(solution)/shard_map/while/body/eval_jaxpr/ppermute | solution.py:9
  277.1 85.8 %all-reduce.2.cloned.1.call-done = f32[64,256]{1,0:T(8,128)} async-done(((f32[64,256]{1,0:T(8,128)}), f32[64,256]{1,0:T(8,128)}) %all-reduce.2.cloned.1.call-update) | async-done | bytes 65552 | tf_op jit(solution)/shard_map/psum | solution.py:66
  (127 shorter events, 69.8 us)
Async XLA Ops:
  6.5 356.4 %all-reduce.2.cloned.1.call-start = ((), (), s32[]{:S(2)}) async-start(), calls=%async_computation | async-start | bytes 131072 | tf_op jit(solution)/shard_map/psum | solution.py:66
  16.9 20.6 %collective-permute-start.2 = (bf16[64,1536]{1,0:T(8,128)(2,1)S(1)}, bf16[64,1536]{1,0:T(8,128)(2,1)S(1)}, u32[]{:S(2)}, u32[]{:S(2)}) collective-permute-start(bf16[64,1536]{1,0:T(8,128)(2,1)S(1)} %all_gather.6), channel_id=1, source_target_pairs={{0,4},{4,8},{8,12},{12,16},{16,20},{20,24},{24,28},{28,32},{32,36}... | collective-permute-start | bytes 589832 | tf_op jit(solution)/shard_map/ppermute | solution.py:9
  16.9 39.0 %collective-permute-start.3 = (bf16[64,1536]{1,0:T(8,128)(2,1)S(1)}, bf16[64,1536]{1,0:T(8,128)(2,1)S(1)}, u32[]{:S(2)}, u32[]{:S(2)}) collective-permute-start(bf16[64,1536]{1,0:T(8,128)(2,1)S(1)} %all_gather.6), channel_id=1, source_target_pairs={{0,8},{4,12},{8,16},{12,20},{16,24},{20,28},{24,32},{28,36},{32,40... | collective-permute-start | bytes 589832 | tf_op jit(solution)/shard_map/ppermute | solution.py:9
  30.0 25.6 %collective-permute-start.6 = (bf16[64,12]{0,1:T(8,128)(2,1)S(1)}, bf16[64,12]{0,1:T(8,128)(2,1)S(1)}, u32[]{:S(2)}, u32[]{:S(2)}) collective-permute-start(bf16[64,12]{0,1:T(8,128)(2,1)S(1)} %bitcast.50), channel_id=1, source_target_pairs={{0,8},{4,12},{8,16},{12,20},{16,24},{20,28},{24,32},{28,36},{32,40... | collective-permute-start | bytes 4616 | tf_op jit(solution)/shard_map/ppermute | solution.py:9
  37.6 18.1 %collective-permute-start.7 = (bf16[64,12]{0,1:T(8,128)(2,1)S(1)}, bf16[64,12]{0,1:T(8,128)(2,1)S(1)}, u32[]{:S(2)}, u32[]{:S(2)}) collective-permute-start(bf16[64,12]{0,1:T(8,128)(2,1)S(1)} %collective-permute-done.5), channel_id=1, source_target_pairs={{0,8},{4,12},{8,16},{12,20},{16,24},{20,28},{24,32},{28,36},{32,40... | collective-permute-start | bytes 4616 | tf_op jit(solution)/shard_map/ppermute | solution.py:9
  37.6 18.4 %collective-permute-start.4 = (bf16[64,1536]{1,0:T(8,128)(2,1)S(1)}, bf16[64,1536]{1,0:T(8,128)(2,1)S(1)}, u32[]{:S(2)}, u32[]{:S(2)}) collective-permute-start(bf16[64,1536]{1,0:T(8,128)(2,1)S(1)} %collective-permute-done.2), channel_id=1, source_target_pairs={{0,8},{4,12},{8,16},{12,20},{16,24},{20,28},{24,32},{28,36},{32,40... | collective-permute-start | bytes 589832 | tf_op jit(solution)/shard_map/ppermute | solution.py:9
  56.9 14.9 %collective-permute-start.1 = (bf16[64,1536]{1,0:T(8,128)(2,1)S(1)}, bf16[64,1536]{1,0:T(8,128)(2,1)S(1)}, u32[]{:S(2)}, u32[]{:S(2)}) collective-permute-start(bf16[64,1536]{1,0:T(8,128)(2,1)S(1)} %get-tuple-element.234), channel_id=1, source_target_pairs={{0,16},{4,20},{8,24},{12,28},{16,32},{20,36},{24,40},{28,44},{32,4... | collective-permute-start | bytes 589832 | tf_op jit(solution)/shard_map/while/body/eval_jaxpr/ppermute | solution.py:9
  59.4 12.3 %collective-permute-start = (bf16[64,12]{1,0:T(8,128)(2,1)S(1)}, bf16[64,12]{1,0:T(8,128)(2,1)S(1)}, u32[]{:S(2)}, u32[]{:S(2)}) collective-permute-start(bf16[64,12]{1,0:T(8,128)(2,1)S(1)} %get-tuple-element.235), channel_id=1, source_target_pairs={{0,16},{4,20},{8,24},{12,28},{16,32},{20,36},{24,40},{28,44},{32,4... | collective-permute-start | bytes 4616 | tf_op jit(solution)/shard_map/while/body/eval_jaxpr/ppermute | solution.py:9
  73.4 17.6 %collective-permute-start.1 = (bf16[64,1536]{1,0:T(8,128)(2,1)S(1)}, bf16[64,1536]{1,0:T(8,128)(2,1)S(1)}, u32[]{:S(2)}, u32[]{:S(2)}) collective-permute-start(bf16[64,1536]{1,0:T(8,128)(2,1)S(1)} %get-tuple-element.234), channel_id=1, source_target_pairs={{0,16},{4,20},{8,24},{12,28},{16,32},{20,36},{24,40},{28,44},{32,4... | collective-permute-start | bytes 589832 | tf_op jit(solution)/shard_map/while/body/eval_jaxpr/ppermute | solution.py:9
  74.2 16.8 %collective-permute-start = (bf16[64,12]{1,0:T(8,128)(2,1)S(1)}, bf16[64,12]{1,0:T(8,128)(2,1)S(1)}, u32[]{:S(2)}, u32[]{:S(2)}) collective-permute-start(bf16[64,12]{1,0:T(8,128)(2,1)S(1)} %get-tuple-element.235), channel_id=1, source_target_pairs={{0,16},{4,20},{8,24},{12,28},{16,32},{20,36},{24,40},{28,44},{32,4... | collective-permute-start | bytes 4616 | tf_op jit(solution)/shard_map/while/body/eval_jaxpr/ppermute | solution.py:9
  92.7 12.5 %collective-permute-start.1 = (bf16[64,1536]{1,0:T(8,128)(2,1)S(1)}, bf16[64,1536]{1,0:T(8,128)(2,1)S(1)}, u32[]{:S(2)}, u32[]{:S(2)}) collective-permute-start(bf16[64,1536]{1,0:T(8,128)(2,1)S(1)} %get-tuple-element.234), channel_id=1, source_target_pairs={{0,16},{4,20},{8,24},{12,28},{16,32},{20,36},{24,40},{28,44},{32,4... | collective-permute-start | bytes 589832 | tf_op jit(solution)/shard_map/while/body/eval_jaxpr/ppermute | solution.py:9
  92.8 12.4 %collective-permute-start = (bf16[64,12]{1,0:T(8,128)(2,1)S(1)}, bf16[64,12]{1,0:T(8,128)(2,1)S(1)}, u32[]{:S(2)}, u32[]{:S(2)}) collective-permute-start(bf16[64,12]{1,0:T(8,128)(2,1)S(1)} %get-tuple-element.235), channel_id=1, source_target_pairs={{0,16},{4,20},{8,24},{12,28},{16,32},{20,36},{24,40},{28,44},{32,4... | collective-permute-start | bytes 4616 | tf_op jit(solution)/shard_map/while/body/eval_jaxpr/ppermute | solution.py:9
  106.9 11.9 %collective-permute-start.1 = (bf16[64,1536]{1,0:T(8,128)(2,1)S(1)}, bf16[64,1536]{1,0:T(8,128)(2,1)S(1)}, u32[]{:S(2)}, u32[]{:S(2)}) collective-permute-start(bf16[64,1536]{1,0:T(8,128)(2,1)S(1)} %get-tuple-element.234), channel_id=1, source_target_pairs={{0,16},{4,20},{8,24},{12,28},{16,32},{20,36},{24,40},{28,44},{32,4... | collective-permute-start | bytes 589832 | tf_op jit(solution)/shard_map/while/body/eval_jaxpr/ppermute | solution.py:9
  120.5 11.8 %collective-permute-start.1 = (bf16[64,1536]{1,0:T(8,128)(2,1)S(1)}, bf16[64,1536]{1,0:T(8,128)(2,1)S(1)}, u32[]{:S(2)}, u32[]{:S(2)}) collective-permute-start(bf16[64,1536]{1,0:T(8,128)(2,1)S(1)} %get-tuple-element.234), channel_id=1, source_target_pairs={{0,16},{4,20},{8,24},{12,28},{16,32},{20,36},{24,40},{28,44},{32,4... | collective-permute-start | bytes 589832 | tf_op jit(solution)/shard_map/while/body/eval_jaxpr/ppermute | solution.py:9
  174.3 12.6 %collective-permute-start.1 = (bf16[64,1536]{1,0:T(8,128)(2,1)S(1)}, bf16[64,1536]{1,0:T(8,128)(2,1)S(1)}, u32[]{:S(2)}, u32[]{:S(2)}) collective-permute-start(bf16[64,1536]{1,0:T(8,128)(2,1)S(1)} %get-tuple-element.234), channel_id=1, source_target_pairs={{0,16},{4,20},{8,24},{12,28},{16,32},{20,36},{24,40},{28,44},{32,4... | collective-permute-start | bytes 589832 | tf_op jit(solution)/shard_map/while/body/eval_jaxpr/ppermute | solution.py:9
  175.1 11.8 %collective-permute-start = (bf16[64,12]{1,0:T(8,128)(2,1)S(1)}, bf16[64,12]{1,0:T(8,128)(2,1)S(1)}, u32[]{:S(2)}, u32[]{:S(2)}) collective-permute-start(bf16[64,12]{1,0:T(8,128)(2,1)S(1)} %get-tuple-element.235), channel_id=1, source_target_pairs={{0,16},{4,20},{8,24},{12,28},{16,32},{20,36},{24,40},{28,44},{32,4... | collective-permute-start | bytes 4616 | tf_op jit(solution)/shard_map/while/body/eval_jaxpr/ppermute | solution.py:9
  188.6 13.7 %collective-permute-start.1 = (bf16[64,1536]{1,0:T(8,128)(2,1)S(1)}, bf16[64,1536]{1,0:T(8,128)(2,1)S(1)}, u32[]{:S(2)}, u32[]{:S(2)}) collective-permute-start(bf16[64,1536]{1,0:T(8,128)(2,1)S(1)} %get-tuple-element.234), channel_id=1, source_target_pairs={{0,16},{4,20},{8,24},{12,28},{16,32},{20,36},{24,40},{28,44},{32,4... | collective-permute-start | bytes 589832 | tf_op jit(solution)/shard_map/while/body/eval_jaxpr/ppermute | solution.py:9
  188.7 13.6 %collective-permute-start = (bf16[64,12]{1,0:T(8,128)(2,1)S(1)}, bf16[64,12]{1,0:T(8,128)(2,1)S(1)}, u32[]{:S(2)}, u32[]{:S(2)}) collective-permute-start(bf16[64,12]{1,0:T(8,128)(2,1)S(1)} %get-tuple-element.235), channel_id=1, source_target_pairs={{0,16},{4,20},{8,24},{12,28},{16,32},{20,36},{24,40},{28,44},{32,4... | collective-permute-start | bytes 4616 | tf_op jit(solution)/shard_map/while/body/eval_jaxpr/ppermute | solution.py:9
  204.1 13.4 %collective-permute-start.1 = (bf16[64,1536]{1,0:T(8,128)(2,1)S(1)}, bf16[64,1536]{1,0:T(8,128)(2,1)S(1)}, u32[]{:S(2)}, u32[]{:S(2)}) collective-permute-start(bf16[64,1536]{1,0:T(8,128)(2,1)S(1)} %get-tuple-element.234), channel_id=1, source_target_pairs={{0,16},{4,20},{8,24},{12,28},{16,32},{20,36},{24,40},{28,44},{32,4... | collective-permute-start | bytes 589832 | tf_op jit(solution)/shard_map/while/body/eval_jaxpr/ppermute | solution.py:9
  204.1 13.3 %collective-permute-start = (bf16[64,12]{1,0:T(8,128)(2,1)S(1)}, bf16[64,12]{1,0:T(8,128)(2,1)S(1)}, u32[]{:S(2)}, u32[]{:S(2)}) collective-permute-start(bf16[64,12]{1,0:T(8,128)(2,1)S(1)} %get-tuple-element.235), channel_id=1, source_target_pairs={{0,16},{4,20},{8,24},{12,28},{16,32},{20,36},{24,40},{28,44},{32,4... | collective-permute-start | bytes 4616 | tf_op jit(solution)/shard_map/while/body/eval_jaxpr/ppermute | solution.py:9
  219.2 14.4 %collective-permute-start.1 = (bf16[64,1536]{1,0:T(8,128)(2,1)S(1)}, bf16[64,1536]{1,0:T(8,128)(2,1)S(1)}, u32[]{:S(2)}, u32[]{:S(2)}) collective-permute-start(bf16[64,1536]{1,0:T(8,128)(2,1)S(1)} %get-tuple-element.234), channel_id=1, source_target_pairs={{0,16},{4,20},{8,24},{12,28},{16,32},{20,36},{24,40},{28,44},{32,4... | collective-permute-start | bytes 589832 | tf_op jit(solution)/shard_map/while/body/eval_jaxpr/ppermute | solution.py:9
  219.3 14.3 %collective-permute-start = (bf16[64,12]{1,0:T(8,128)(2,1)S(1)}, bf16[64,12]{1,0:T(8,128)(2,1)S(1)}, u32[]{:S(2)}, u32[]{:S(2)}) collective-permute-start(bf16[64,12]{1,0:T(8,128)(2,1)S(1)} %get-tuple-element.235), channel_id=1, source_target_pairs={{0,16},{4,20},{8,24},{12,28},{16,32},{20,36},{24,40},{28,44},{32,4... | collective-permute-start | bytes 4616 | tf_op jit(solution)/shard_map/while/body/eval_jaxpr/ppermute | solution.py:9
  235.3 12.5 %collective-permute-start.1 = (bf16[64,1536]{1,0:T(8,128)(2,1)S(1)}, bf16[64,1536]{1,0:T(8,128)(2,1)S(1)}, u32[]{:S(2)}, u32[]{:S(2)}) collective-permute-start(bf16[64,1536]{1,0:T(8,128)(2,1)S(1)} %get-tuple-element.234), channel_id=1, source_target_pairs={{0,16},{4,20},{8,24},{12,28},{16,32},{20,36},{24,40},{28,44},{32,4... | collective-permute-start | bytes 589832 | tf_op jit(solution)/shard_map/while/body/eval_jaxpr/ppermute | solution.py:9
  235.4 12.4 %collective-permute-start = (bf16[64,12]{1,0:T(8,128)(2,1)S(1)}, bf16[64,12]{1,0:T(8,128)(2,1)S(1)}, u32[]{:S(2)}, u32[]{:S(2)}) collective-permute-start(bf16[64,12]{1,0:T(8,128)(2,1)S(1)} %get-tuple-element.235), channel_id=1, source_target_pairs={{0,16},{4,20},{8,24},{12,28},{16,32},{20,36},{24,40},{28,44},{32,4... | collective-permute-start | bytes 4616 | tf_op jit(solution)/shard_map/while/body/eval_jaxpr/ppermute | solution.py:9
  (14 other events, 149.6 us)
Sparse Core Ops, SparseCore 0:
  277.2 85.6 all-reduce.1
where the time goes:
time: 372 us; the launch traced here: 371 us
  waiting for transfers between devices  239 us (64%)
  starting transfers between devices  54.3 us (15%)
  local copies, waits for them, and re-layouts  23 us (6%)
  matrix products  22.6 us (6%)
  blocking collectives  17.7 us (5%)
  between operations  13.5 us (4%)
    ppermute x36, waiting for transfers between devices, passed_along(): return lax.ppermute(x, axis, [(i, (i + by) % size) for i in range(size)])  153 us
    psum x1, waiting for transfers between devices, per_device(): product = lax.psum(running, 'team')  85.8 us
    ppermute x36, starting transfers between devices, passed_along(): return lax.ppermute(x, axis, [(i, (i + by) % size) for i in range(size)])  54.3 us
    dot_general x16, matrix products, contribute(): lax.dot_general(scaled, cov_slab, (((1,), (1,)), ((), ())), preferred_ele...  22.6 us
    unnamed x5, local copies, waits for them, and re-layouts  15.1 us
    all_gather x1, blocking collectives, per_device(): lax.all_gather(loadings, 'team', axis=1, tiled=True)  10.4 us
  transfers between devices with their start and end apart: 37, of which 17 were waited for; matrix products, arithmetic and copies ran while one was open for 5% of the time, Pallas kernels for 0%

commit v1 on v0

v1 whole, which is shorter than its diff:
```python
import jax
import jax.numpy as jnp
from jax import lax
from jax.sharding import PartitionSpec as P


def per_device(loadings, scales, cov):
    n_loads, width = loadings.shape
    groups = scales.shape[1]
    team_size = lax.axis_size("team")
    blk_size = lax.axis_size("blk")
    scaled = (
        loadings.astype(jnp.float32).reshape(n_loads, groups, width // groups)
        * scales.astype(jnp.float32)[:, :, None]
    ).reshape(n_loads, width).astype(jnp.bfloat16)
    pairs = []
    for b in range(blk_size):
        c, d = divmod(b, team_size)
        for p in range(team_size):
            pairs.append((b * team_size + p, (c * team_size + p) * team_size + d))
    moved = lax.ppermute(scaled, ("blk", "team"), pairs)
    gathered = lax.all_gather(moved, "blk", axis=1, tiled=True)
    stops = cov.shape[1]
    gathered = gathered.reshape(n_loads, stops, cov.shape[3])
    cov_local = cov[:, :, 0, :]
    part = lax.dot_general(
        gathered, cov_local, (((1, 2), (1, 2)), ((), ())), preferred_element_type=jnp.float32
    )
    return lax.psum(part, "team")


def solution(mesh):
    placed = (P(None, ("blk", "team")), P(None, ("blk", "team")), P("blk", None, "team", None))
    return jax.shard_map(
        per_device, mesh=mesh, in_specs=placed, out_specs=P(None, "blk"), check_vma=False
    )
```

time: 372 us -> 395 us (1.062)
  waiting for transfers between devices: 239 us -> 353 us
  starting transfers between devices: 54.3 us -> 4.98 us
  local copies, waits for them, and re-layouts: 23 us -> 2.99 us
  blocking collectives: 17.7 us -> 0 us
    all_gather x0 -> x1, waiting for transfers between devices: none -> 266 us  [per_device(): gathered = lax.all_gather(moved, 'blk', axis=1, tiled=True)]
    ppermute x36 -> x1, waiting for transfers between devices: 153 us -> 1.76 us  [per_device(): moved = lax.ppermute(scaled, ('blk', 'team'), pairs)]
    ppermute x36 -> x1, starting transfers between devices: 54.3 us -> 4.94 us  [per_device(): moved = lax.ppermute(scaled, ('blk', 'team'), pairs)]
    all_gather x2 -> x0, blocking collectives: 17.7 us -> none  [the longest x1 10.4 us: per_device(): lax.all_gather(loadings, 'team', axis=1, tiled=True)]
    unnamed x5 -> x3, local copies, waits for them, and re-layouts: 15.1 us -> 2.09 us
    dynamic_slice x1 -> x0, local copies, waits for them, and re-layouts: 4.4 us -> none  [contribute(): lax.dynamic_index_in_dim(cov_local, jnp.mod(stop_num, cycle_stops), 1, ke...]
    dot_general x16 -> x1, matrix products: 22.6 us -> 19.6 us  [per_device(): lax.dot_general(gathered, cov_local, (((1, 2), (1, 2)), ((), ())), prefer...]
  transfers between devices with their start and end apart: 37 -> 3, of which waited for: 17 -> 3; matrix products, arithmetic and copies ran while one was open for 5% -> 0% of each run, Pallas kernels for 0% -> 0%
where the time goes in v1:
time: 395 us
  waiting for transfers between devices  353 us (89%)
  matrix products  19.6 us (5%)
  between operations  13.4 us (3%)
  starting transfers between devices  4.98 us (1%)
    all_gather x1, waiting for transfers between devices, per_device(): gathered = lax.all_gather(moved, 'blk', axis=1, tiled=True)  266 us
    psum x1, waiting for transfers between devices, per_device(): return lax.psum(part, 'team')  85.7 us
    dot_general x1, matrix products, per_device(): lax.dot_general(gathered, cov_local, (((1, 2), (1, 2)), ((), ())), prefer...  19.6 us
  transfers between devices with their start and end apart: 3, of which 3 were waited for; matrix products, arithmetic and copies ran while one was open for 0% of the time, Pallas kernels for 0%

profile of v1, /device:TPU:1, one launch (start us, length us, event | category | flops | bytes accessed | tf_op | source)
XLA Modules:
  0.0 395.1 jit_solution(3153705874606790821)
XLA Ops:
  6.5 0.0 all-gather.2.cloned.1.call-start
  6.5 0.8 copy.6
  7.3 0.1 mul.11
  7.4 0.8 fusion.9
  8.3 4.9 %collective-permute-start = (bf16[64,384]{1,0:T(8,128)(2,1)S(1)}, bf16[64,384]{1,0:T(8,128)(2,1)S(1)}, u32[]{:S(2)}, u32[]{:S(2)}) collective-permute-start(bf16[64,384]{1,0:T(8,128)(2,1)S(1)} %fusion.9), channel_id=1, source_target_pairs={{0,0},{1,4},{2,8},{3,12},{4,1},{5,5},{6,9},{7,13},{8,2},{9,6},{10,... | collective-permute-start | bytes 147464 | tf_op jit(solution)/shard_map/ppermute | solution.py:21
  13.2 1.8 collective-permute-done
  15.0 0.0 copy-start
  15.0 0.6 copy-done
  15.6 0.0 all-gather.2.cloned.1.call-update
  15.6 0.0 all-reduce.2.cloned.1.call-start
  15.7 265.7 %all-gather.2.cloned.1.call-done = bf16[64,24576]{1,0:T(8,128)(2,1)} async-done(((bf16[64,384]{1,0:T(8,128)(2,1)}), bf16[64,24576]{1,0:T(8,128)(2,1)}) %all-gather.2.cloned.1.call-update) | async-done | bytes 3145744 | tf_op jit(solution)/shard_map/all_gather | solution.py:22
  281.4 19.6 %fusion.4 = f32[64,256]{1,0:T(8,128)} fusion(bf16[256,16,1536]{2,1,0:T(8,128)(2,1)} %bitcast.15, bf16[8,16,8,1536]{3,2,1,0:T(8,128)(2,1)} %bitcast.16), kind=kOutput, calls=%fused_computation.4 | convolution fusion | flops 805306368 | bytes 15794176 | tf_op jit(solution)/shard_map/dot_general | solution.py:26
  301.0 0.0 all-reduce.2.cloned.1.call-update
  301.1 85.7 %all-reduce.2.cloned.1.call-done = f32[64,256]{1,0:T(8,128)} async-done(((f32[64,256]{1,0:T(8,128)}), f32[64,256]{1,0:T(8,128)}) %all-reduce.2.cloned.1.call-update) | async-done | bytes 65552 | tf_op jit(solution)/shard_map/psum | solution.py:29
  386.7 1.5 copy.23
Async XLA Ops:
  6.5 274.9 %all-gather.2.cloned.1.call-start = ((), (), s32[]{:S(2)}) async-start(), calls=%async_computation | async-start | bytes 3194880 | tf_op jit(solution)/shard_map/all_gather | solution.py:22
  8.3 6.7 %collective-permute-start = (bf16[64,384]{1,0:T(8,128)(2,1)S(1)}, bf16[64,384]{1,0:T(8,128)(2,1)S(1)}, u32[]{:S(2)}, u32[]{:S(2)}) collective-permute-start(bf16[64,384]{1,0:T(8,128)(2,1)S(1)} %fusion.9), channel_id=1, source_target_pairs={{0,0},{1,4},{2,8},{3,12},{4,1},{5,5},{6,9},{7,13},{8,2},{9,6},{10,... | collective-permute-start | bytes 147464 | tf_op jit(solution)/shard_map/ppermute | solution.py:21
  15.0 0.6 copy-start
  15.6 371.1 %all-reduce.2.cloned.1.call-start = ((), (), s32[]{:S(2)}) async-start(), calls=%async_computation.1 | async-start | bytes 131072 | tf_op jit(solution)/shard_map/psum | solution.py:29
Sparse Core Ops, SparseCore 0:
  15.7 265.6 all-gather.1
  301.2 85.5 all-reduce.1
